TPU v7x, 128 devices: a whole 4x4x4 slice. The times are simulated.
128 devices in a mesh: seq: 32 (over z, y, core), tp: 4 (over x).
Axes of the slice: x: 4, y: 4, z: 4, core: 2. Of those that a mesh axis runs over, the one named last changes fastest.
Arguments:
- hidden: bfloat16 [32768, 2048], P('seq', 'tp'), may hold values from -6 to 6
- x_weight: bfloat16 [2048, 4096], P(None, 'tp'), may hold values from -0.125 to 0.125
- z_weight: bfloat16 [2048, 4096], P(None, 'tp'), may hold values from -0.125 to 0.125
- bc_weight: bfloat16 [2048, 256], P(None, 'tp'), may hold values from -0.125 to 0.125
- dt_weight: bfloat16 [2048, 64], P(None, 'tp'), may hold values from -0.125 to 0.125
- conv_x: float32 [4, 4096], P(None, 'tp'), may hold values from -3 to 3
- conv_bc: float32 [4, 256], replicated, may hold values from -3 to 3
- dt_bias: float32 [64], P('tp'), may hold values from -2 to 1
- decay_rate: float32 [64], P('tp'), may hold values from 2e-05 to 0.2
- skip_gain: float32 [64], P('tp'), may hold values from 0.2 to 1.5
- norm_gain: float32 [4096], P('tp'), may hold values from 0.5 to 1.5
- out_weight: bfloat16 [4096, 2048], P('tp'), may hold values from -0.09375 to 0.09375
- lengths: int32 [4], replicated, may hold values from 1 to 16384, as said below
- owners: int32 [32], P('seq'), may hold values from 0 to 3, as said below
Outputs:
- mixed: bfloat16 [32768, 2048], P('seq', 'tp')
- final_state: float32 [32, 64, 64, 128], P('seq', 'tp')
- conv_edge_x: bfloat16 [32, 3, 4096], P('seq', None, 'tp')
- conv_edge_bc: bfloat16 [32, 3, 256], P('seq')
Inputs may be any that keep to these rules, and one draw needn't show every extreme that they name: The prompts are packed in order and their lengths sum to 32768; the second prompt is the longest and holds exactly half of 32768 tokens; the third and fourth together hold at least 3 tokens, and one of them holds one or two. `owners`: every prompt is kept by the same number of indices.
All inputs are finite; a program needn't handle non-finite values.
Results may differ from a plain program's by a relative error of at most 0.013.
Values may be sent and summed in bfloat16 or wider, within the bound.
No kernel may reach another device: no remote copies, remote signals or barrier semaphores. Data moves between devices by JAX's collectives and lax.ppermute only.
A program may use at most 192 MiB of HBM per device.

v0:
```python
import jax
import jax.numpy as jnp
from jax import lax
from jax.sharding import PartitionSpec as P

NS = 128
KCONV = 4
GROUP = 256
PROMPTS = 4
DIN = 4096
highest = lax.Precision.HIGHEST
epsilon = 1e-05


def passed_along(block, axis, distance):
    devices = range(lax.axis_size(axis))
    route = [(i - distance, i) for i in devices if i - distance in devices]
    return lax.ppermute(block, axis, route)


def prefix(value, axis, join, neutral):
    count, mine = (lax.axis_size(axis), lax.axis_index(axis))
    pieces = jax.tree.map(lambda part: lax.all_gather(part, axis), value)
    running = jax.tree.map(
        lambda part, zero: jnp.full_like(part, 0) + jnp.asarray(zero, part.dtype), value, neutral
    )

    def lap(position, running):
        longer = join(running, jax.tree.map(lambda part: part[position], pieces))
        return jax.tree.map(lambda new, old: jnp.where(position < mine, new, old), longer, running)

    return lax.fori_loop(0, count - 1, lap, running)


def segment_of(positions, prompt_end):
    counted = jnp.sum((positions[:, None] >= prompt_end[None, :]).astype(jnp.int32), axis=1)
    return jnp.where(positions < 0, -1, counted)


def short_conv(extended, seg_ext, kernel):
    taps = kernel.shape[0]
    count = extended.shape[0] - taps + 1
    total = jnp.zeros((count, extended.shape[1]), jnp.float32)
    for offset in range(taps):
        same = (seg_ext[offset : offset + count] == seg_ext[taps - 1 :]).astype(jnp.float32)
        total = (
            total
            + extended[offset : offset + count].astype(jnp.float32)
            * kernel[offset][None, :]
            * same[:, None]
        )
    return jax.nn.silu(total).astype(jnp.bfloat16)


def advance_block(state, block):
    x_blk, b_blk, c_blk, dt_blk, log_blk, seg_blk, seg_prior = block
    length = seg_blk.shape[0]
    acum = jnp.cumsum(log_blk, axis=0)
    index = jnp.arange(length, dtype=jnp.int32)
    keep = (seg_blk[:, None] == seg_blk[None, :]) & (index[:, None] >= index[None, :])
    spread = acum[:, None, :] - acum[None, :, :]
    decay = jnp.where(keep[:, :, None], jnp.exp(jnp.where(keep[:, :, None], spread, 0.0)), 0.0)
    scores = jnp.dot(c_blk, b_blk.T, precision=highest)
    mixing = scores[:, :, None] * decay * dt_blk[None, :, :]
    output = jnp.einsum("ijh,jhp->ihp", mixing, x_blk, precision=highest)
    inflow = jnp.where((seg_blk == seg_prior)[:, None], jnp.exp(acum), 0.0)
    output = output + inflow[:, :, None] * jnp.einsum(
        "in,hpn->ihp", c_blk, state, precision=highest
    )
    closing = seg_blk[length - 1]
    tail = (
        jnp.where((seg_blk == closing)[:, None], jnp.exp(acum[length - 1][None, :] - acum), 0.0)
        * dt_blk
    )
    fresh = jnp.einsum("jh,jhp,jn->hpn", tail, x_blk, b_blk, precision=highest)
    carry = jnp.where(closing == seg_prior, jnp.exp(acum[length - 1]), 0.0)
    return (carry[:, None, None] * state + fresh, (output, state))


def state_at(start_state, seg_prior, x_rows, b_rows, dt_rows, log_rows, seg_rows, inner, prompt):
    acum = jnp.cumsum(log_rows, axis=0)
    level = acum[inner]
    index = jnp.arange(seg_rows.shape[0], dtype=jnp.int32)
    chosen = (seg_rows == prompt) & (index <= inner)
    weight = (
        jnp.where(
            chosen[:, None], jnp.exp(jnp.where(chosen[:, None], level[None, :] - acum, 0.0)), 0.0
        )
        * dt_rows
    )
    inflow = jnp.where(seg_rows[inner] == seg_prior, jnp.exp(level), 0.0)
    return inflow[:, None, None] * start_state + jnp.einsum(
        "jh,jhp,jn->hpn", weight, x_rows, b_rows, precision=highest
    )


def per_device(
    hidden,
    x_weight,
    z_weight,
    bc_weight,
    dt_weight,
    conv_x,
    conv_bc,
    dt_bias,
    decay_rate,
    skip_gain,
    norm_gain,
    out_weight,
    lengths,
    owners,
):
    rows_here = hidden.shape[0]
    width_here = x_weight.shape[1]
    heads_here = dt_bias.shape[0]
    head_width = width_here // heads_here
    my_index = lax.axis_index("seq")
    first_row = my_index * rows_here
    prompt_end = jnp.cumsum(lengths)
    prompt_start = prompt_end - lengths
    positions = first_row + jnp.arange(rows_here, dtype=jnp.int32)
    segment = segment_of(positions, prompt_end)
    bc_full = lax.all_gather(bc_weight, "tp", axis=1, tiled=True)
    piece = lax.all_gather(hidden, "tp", axis=1, tiled=True)

    def take(matrix):
        return jnp.dot(piece, matrix, preferred_element_type=jnp.float32)

    x_acc = take(x_weight)
    z_acc = take(z_weight)
    dt_raw = take(dt_weight)
    bc_acc = take(bc_full)
    x_in = x_acc.astype(jnp.bfloat16)
    z_in = z_acc.astype(jnp.bfloat16)
    bc_in = bc_acc.astype(jnp.bfloat16)
    joined = jnp.concatenate([x_in, bc_in], axis=1)
    earlier = passed_along(joined[rows_here - (KCONV - 1) :], "seq", 1)
    extended = jnp.concatenate([earlier, joined], axis=0)
    seg_ext = jnp.concatenate(
        [
            segment_of(
                first_row - (KCONV - 1) + jnp.arange(KCONV - 1, dtype=jnp.int32), prompt_end
            ),
            segment,
        ]
    )
    kernel = jnp.concatenate([conv_x, conv_bc], axis=1)
    mixed_in = short_conv(extended, seg_ext, kernel)
    x_conv = mixed_in[:, :width_here].astype(jnp.float32).reshape(rows_here, heads_here, head_width)
    b_conv = mixed_in[:, width_here : width_here + NS].astype(jnp.float32)
    c_conv = mixed_in[:, width_here + NS :].astype(jnp.float32)
    step_size = jax.nn.softplus(dt_raw + dt_bias[None, :])
    log_decay = -decay_rate[None, :] * step_size
    blocks = rows_here // GROUP
    block_first = first_row + jnp.arange(blocks, dtype=jnp.int32) * GROUP
    seg_prior = segment_of(block_first - 1, prompt_end)
    packed = (
        x_conv.reshape(blocks, GROUP, heads_here, head_width),
        b_conv.reshape(blocks, GROUP, NS),
        c_conv.reshape(blocks, GROUP, NS),
        step_size.reshape(blocks, GROUP, heads_here),
        log_decay.reshape(blocks, GROUP, heads_here),
        segment.reshape(blocks, GROUP),
        seg_prior,
    )
    init_state = jnp.zeros((heads_here, head_width, NS), jnp.float32)
    local_end, (outputs, priors) = lax.scan(advance_block, init_state, packed)
    device_prior = seg_prior[0]
    level = jnp.cumsum(log_decay, axis=0)
    through = jnp.where(segment[rows_here - 1] == device_prior, jnp.exp(level[rows_here - 1]), 0.0)

    def link(earlier_pair, later_pair):
        return (
            earlier_pair[0] * later_pair[0],
            later_pair[0][:, None, None] * earlier_pair[1] + later_pair[1],
        )

    unused, entering = prefix(
        (through, local_end), "seq", link, (jnp.ones_like(through), jnp.zeros_like(local_end))
    )
    inflow = jnp.where((segment == device_prior)[:, None], jnp.exp(level), 0.0)
    ssm = outputs.reshape(rows_here, heads_here, head_width)
    ssm = ssm + inflow[:, :, None] * jnp.einsum("in,hpn->ihp", c_conv, entering, precision=highest)
    ssm = ssm + skip_gain[None, :, None] * x_conv
    gated = ssm.reshape(rows_here, width_here) * jax.nn.silu(z_in.astype(jnp.float32))
    square_sum = lax.psum(jnp.sum(gated * gated, axis=1), "tp")
    normed = (gated * lax.rsqrt(square_sum / DIN + epsilon)[:, None] * norm_gain[None, :]).astype(
        jnp.bfloat16
    )
    mixed_cols = lax.psum_scatter(
        lax.dot_general(
            out_weight, normed, (((0,), (1,)), ((), ())), preferred_element_type=jnp.float32
        ),
        "tp",
        scatter_dimension=0,
        tiled=True,
    )
    mixed = mixed_cols.T.astype(jnp.bfloat16)
    last_row = prompt_end - 1
    holder = last_row // rows_here
    present = holder == my_index
    inner = jnp.clip(last_row - first_row, 0, rows_here - 1)

    def finish(prompt_id, inner_row):
        return state_at(
            entering,
            device_prior,
            x_conv,
            b_conv,
            step_size,
            log_decay,
            segment,
            inner_row,
            prompt_id,
        )

    finals = jax.vmap(finish)(jnp.arange(PROMPTS, dtype=jnp.int32), inner)
    finals = jnp.where(present[:, None, None, None], finals, 0.0)

    def edge_of(inner_row, start_row, end_row):
        window = lax.dynamic_slice_in_dim(extended, inner_row + 1, KCONV - 1, 0)
        rows_global = end_row - (KCONV - 2) + jnp.arange(KCONV - 1, dtype=jnp.int32)
        return jnp.where((rows_global >= start_row)[:, None], window, jnp.zeros_like(window))

    edges = jax.vmap(edge_of)(inner, prompt_start, last_row)
    edges = jnp.where(present[:, None, None], edges.astype(jnp.float32), 0.0)
    finals_all, edges_all = lax.psum((finals, edges), "seq")
    keeper = owners[0]
    final_state = finals_all[keeper][None]
    kept_edges = edges_all[keeper]
    conv_edge_x = kept_edges[:, :width_here].astype(jnp.bfloat16)[None]
    conv_edge_bc = kept_edges[:, width_here:].astype(jnp.bfloat16)[None]
    return (mixed, final_state, conv_edge_x, conv_edge_bc)


def solution(mesh):
    return jax.shard_map(
        per_device,
        mesh=mesh,
        in_specs=(
            P("seq", "tp"),
            P(None, "tp"),
            P(None, "tp"),
            P(None, "tp"),
            P(None, "tp"),
            P(None, "tp"),
            P(),
            P("tp"),
            P("tp"),
            P("tp"),
            P("tp"),
            P("tp", None),
            P(),
            P("seq"),
        ),
        out_specs=(
            P("seq", "tp"),
            P("seq", "tp", None, None),
            P("seq", None, "tp"),
            P("seq", None, None),
        ),
        check_vma=False,
    )
```

profile of v0, /device:TPU:1, one launch (start us, length us, event | category | flops | bytes accessed | tf_op | source)
XLA Modules:
  0.0 635.1 jit_solution(17370364813948370289)
XLA Ops:
  12.4 22.5 %all-gather.8.cloned.1.call-done = bf16[2048,256]{0,1:T(8,128)(2,1)} async-done(((bf16[2048,64]{0,1:T(8,128)(2,1)}), bf16[2048,256]{0,1:T(8,128)(2,1)}) %all-gather.8.cloned.1.call-update) | async-done | bytes 1048592 | tf_op jit(solution)/shard_map/all_gather | solution.py:123
  34.9 52.1 %all-gather.6.cloned.1.call-done = bf16[1024,2048]{1,0:T(8,128)(2,1)} async-done(((bf16[1024,512]{1,0:T(8,128)(2,1)}), bf16[1024,2048]{1,0:T(8,128)(2,1)}) %all-gather.6.cloned.1.call-update) | async-done | bytes 4194320 | tf_op jit(solution)/shard_map/all_gather | solution.py:124
  87.0 3.9 convolution_convert_fusion.1
  91.0 7.0 %convolution_convert_fusion = bf16[1024,1024]{0,1:T(8,128)(2,1)S(1)} fusion(bf16[1024,2048]{1,0:T(8,128)(2,1)S(1)} %copy-done.6, bf16[2048,1024]{1,0:T(8,128)(2,1)} %param.19), kind=kOutput, calls=%fused_computation.87 | convolution fusion | flops 4296015872 | bytes 10485760 | tf_op jit(solution)/shard_map/dot_general | solution.py:127
  98.8 3.8 collective-permute-start
  104.0 3.0 collective-permute-done
  107.0 2.8 maximum_maximum_fusion
  109.8 7.4 %multiply_convert_fusion = bf16[1024,1280]{0,1:T(8,128)(2,1)S(1)} fusion(bf16[1024,256]{0,1:T(8,128)(2,1)S(1)} %convolution_convert_fusion.1, bf16[1027,1280]{0,1:T(8,128)(2,1)S(1)} %maximum_maximum_fusion, f32[1280]{0:T(1024)S(1)} %get-tuple-element.304, f32[1024]{0:T(1024)S(1)} %get-tuple-element.360, f32[1280]{0:T(1024)S(1)} %get-tuple-element.305, ...), kind=kLoop, calls=%fused_computation.69 | loop fusion | flops 28835840 | bytes 13139968 | tf_op jit(solution)/shard_map/convert_element_type | solution.py:52
  117.3 1.4 copy-done.5
  118.7 2.4 slice_convert_fusion
  121.6 5.6 reshape_reshape.3
  127.2 162.7 %while.32 = (s32[]{:T(128)}, f32[16,64,128]{2,1,0:T(8,128)S(1)}, f32[4,256,16,64]{1,0,3,2:T(4,128)}, s32[4,256]{1,0:T(4,128)S(1)}, s32[4]{0:T(128)S(1)}, /*index...) while((s32[]{:T(128)}, f32[16,64,128]{2,1,0:T(8,128)S(1)}, ...), condition=%wide.region_7.8_spmd.clone.clone, body=%wide.region_4.7_spmd.clone.sunk.clone | while | flops 1718571520 | bytes 14622798 | solution.py:167
  130.0 1.3 broadcast_compare_fusion.6
  133.1 3.3 constant_dynamic-slice_fusion.14
  136.4 4.9 fusion.121
  144.6 23.4 %dynamic_update_slice.7 = f32[4,256,16,64]{1,0,3,2:T(4,128)} dynamic-update-slice(f32[4,256,16,64]{1,0,3,2:T(4,128)} %get-tuple-element.565, f32[1,256,16,64]{1,0,3,2:T(1,128)S(1)} %copy.168, s32[]{:T(128)S(6)} %copy.175, s32[]{:T(128)} %constant.101.clone.1..sunk.2, s32[]{:T(128)} %constant.101.clone.1..sunk.2, s32[]{:T(128)} %constant.101.clone.1..sunk.2) | dynamic-update-slice | bytes 2097156 | tf_op jit(solution)/shard_map/while/body/jit(dynamic_update_index_in_dim)/dynamic_update_slice | solution.py:167
  170.7 1.3 broadcast_compare_fusion.6
  173.7 3.3 constant_dynamic-slice_fusion.14
  177.0 4.9 fusion.121
  185.3 23.4 %dynamic_update_slice.7 = f32[4,256,16,64]{1,0,3,2:T(4,128)} dynamic-update-slice(f32[4,256,16,64]{1,0,3,2:T(4,128)} %get-tuple-element.565, f32[1,256,16,64]{1,0,3,2:T(1,128)S(1)} %copy.168, s32[]{:T(128)S(6)} %copy.175, s32[]{:T(128)} %constant.101.clone.1..sunk.2, s32[]{:T(128)} %constant.101.clone.1..sunk.2, s32[]{:T(128)} %constant.101.clone.1..sunk.2) | dynamic-update-slice | bytes 2097156 | tf_op jit(solution)/shard_map/while/body/jit(dynamic_update_index_in_dim)/dynamic_update_slice | solution.py:167
  211.3 1.3 broadcast_compare_fusion.6
  214.3 3.3 constant_dynamic-slice_fusion.14
  217.6 4.9 fusion.121
  225.9 23.4 %dynamic_update_slice.7 = f32[4,256,16,64]{1,0,3,2:T(4,128)} dynamic-update-slice(f32[4,256,16,64]{1,0,3,2:T(4,128)} %get-tuple-element.565, f32[1,256,16,64]{1,0,3,2:T(1,128)S(1)} %copy.168, s32[]{:T(128)S(6)} %copy.175, s32[]{:T(128)} %constant.101.clone.1..sunk.2, s32[]{:T(128)} %constant.101.clone.1..sunk.2, s32[]{:T(128)} %constant.101.clone.1..sunk.2) | dynamic-update-slice | bytes 2097156 | tf_op jit(solution)/shard_map/while/body/jit(dynamic_update_index_in_dim)/dynamic_update_slice | solution.py:167
  251.9 1.3 broadcast_compare_fusion.6
  254.9 3.3 constant_dynamic-slice_fusion.14
  258.2 4.9 fusion.121
  266.5 23.4 %dynamic_update_slice.7 = f32[4,256,16,64]{1,0,3,2:T(4,128)} dynamic-update-slice(f32[4,256,16,64]{1,0,3,2:T(4,128)} %get-tuple-element.565, f32[1,256,16,64]{1,0,3,2:T(1,128)S(1)} %copy.168, s32[]{:T(128)S(6)} %copy.175, s32[]{:T(128)} %constant.101.clone.1..sunk.2, s32[]{:T(128)} %constant.101.clone.1..sunk.2, s32[]{:T(128)} %constant.101.clone.1..sunk.2) | dynamic-update-slice | bytes 2097156 | tf_op jit(solution)/shard_map/while/body/jit(dynamic_update_index_in_dim)/dynamic_update_slice | solution.py:167
  293.1 4.5 reduce-window.21
  299.2 24.6 %all-gather.1 = f32[32,1,16]{2,1,0:T(1,128)S(1)} all-gather(f32[1,1,16]{2,1,0:T(1,128)S(1)} %bitcast.252), channel_id=1, replica_groups=mesh['seq'=32,'tp'=4] {'seq'}, dimensions={0}, use_global_device_ids=true | all-gather | bytes 2112 | tf_op jit(solution)/shard_map/all_gather | solution.py:23
  324.0 6.3 reshape.362
  330.4 34.7 %all-gather.10.cloned.1.call-done = f32[512,64,128]{2,1,0:T(8,128)} async-done(((f32[16,64,128]{2,1,0:T(8,128)}), f32[512,64,128]{2,1,0:T(8,128)}) %all-gather.10.cloned.1.call-update) | async-done | bytes 16777232 | tf_op jit(solution)/shard_map/all_gather | solution.py:23
  365.1 37.7 %while.33 = (s32[]{:T(128)}, f32[16,64,128]{2,1,0:T(8,128)S(1)}, s32[]{:T(128)}, f32[32,16]{1,0:T(8,128)S(1)}, f32[32,16,64,128]{3,2,1,0:T(8,128)}) while((s32[]{:T(128)}, f32[16,64,128]{2,1,0:T(8,128)S(1)}, s32[]{:T(128)}, f32[32,16]{1,0:T(8,128)S(1)}, f32[32,16,64,128]{3,2,1,0:T(8,128)}) %tuple.136), condition=%wide.region_11.12_spmd.clone.clone, body=%wide.region_10.11_spmd.clone.sunk.clone | while | flops 524292 | bytes 1573153 | solution.py:32
  402.8 5.9 multiply_add_fusion
  408.8 7.3 %multiply_reduce_fusion = (f32[1024]{0:T(1024)S(1)}, f32[1024,1024]{0,1:T(8,128)}) fusion(bf16[1024,2048]{1,0:T(8,128)(2,1)S(1)} %copy-done.7, bf16[2048,1024]{1,0:T(8,128)(2,1)S(1)} %copy-done.12, f32[1024,16,64]{0,2,1:T(8,128)S(1)} %multiply_add_fusion), kind=kOutput, calls=%fused_computation.76 | convolution fusion | flops 4304403456 | bytes 16781312 | tf_op jit(solution)/shard_map/dot_general | solution.py:127
  416.1 8.5 %psum.21 = f32[1024]{0:T(1024)S(1)} all-reduce(f32[1024]{0:T(1024)S(1)} %get-tuple-element.368), channel_id=1, replica_groups=mesh['seq'=32,'tp'=4] {'tp'}, use_global_device_ids=true, to_apply=%region_13.14 | all-reduce | flops 1024 | bytes 8192 | tf_op jit(solution)/shard_map/psum | solution.py:186
  424.6 11.7 %fusion.47 = f32[4,16,64,128]{3,2,0,1:T(8,128)} fusion(f32[1024,16,64]{0,2,1:T(8,128)} %bitcast.234, f32[1024,16,4]{0,2,1:T(4,128)S(1)} %multiply_bitcast_fusion, f32[16,64,128]{2,1,0:T(8,128)S(1)} %get-tuple-element.153, f32[4,16]{0,1:T(8,128)S(1)} %copy.101, pred[4]{0:T(512)(128)(4,1)S(1)} %fusion.76, bf16[1024,1280]{0,1:T(8,128)(2,1)} %copy-done.5), kind=kOutput, calls=%fused_computation.84 | convolution fusion | flops 6448218112 | bytes 7340292 | tf_op jit(solution)/shard_map/vmap(jh,jhp,jn->hpn)/dot_general | solution.py:92
  436.7 11.4 %convolution_bitcast_fusion = f32[2048,1024]{0,1:T(8,128)} fusion(bf16[1024,2048]{1,0:T(8,128)(2,1)} %param.29, f32[1024,1024]{0,1:T(8,128)} %get-tuple-element.369, f32[1024]{0:T(1024)S(1)} %copy-done.8, f32[1024]{0:T(1024)S(1)} %add_rsqrt_fusion), kind=kOutput, calls=%fused_computation.70 | convolution fusion | flops 4298113024 | bytes 16785408 | tf_op jit(solution)/shard_map/dot_general | solution.py:191
  449.9 3.4 copy.104
  453.3 8.0 %while.31 = (s32[]{:T(128)}, bf16[1027,1280]{1,0:T(8,128)(2,1)}, s32[4,2]{0,1:T(2,128)S(1)}, bf16[4,3,1280]{2,1,0:T(4,128)(2,1)S(1)}) while((s32[]{:T(128)}, bf16[1027,1280]{1,0:T(8,128)(2,1)}, s32[4,2]{0,1:T(2,128)S(1)}, bf16[4,3,1280]{2,1,0:T(4,128)(2,1)S(1)}) %tuple.120), condition=%wide.while_cond.clone, body=%wide.while_body.sunk.clone | while | flops 2 | bytes 18017 | solution.py:221
  453.9 1.4 bitcast_dynamic-update-slice_fusion.3
  455.9 1.4 bitcast_dynamic-update-slice_fusion.3
  457.9 1.4 bitcast_dynamic-update-slice_fusion.3
  459.9 1.4 bitcast_dynamic-update-slice_fusion.3
  461.4 121.7 %psum.23 = bf16[4,3,1280]{2,1,0:T(4,128)(2,1)S(1)} all-reduce(f32[4,3,1280]{2,1,0:T(4,128)S(1)} %convert_select_fusion), channel_id=1, replica_groups=mesh['seq'=32,'tp'=4] {'seq'}, use_global_device_ids=true, to_apply=%region_16.17 | all-reduce | flops 15360 | bytes 92160 | tf_op jit(solution)/shard_map/psum | solution.py:227
  584.3 1.9 dynamic-slice_bitcast_fusion.1
  586.2 39.4 %reduce-scatter.2.cloned.1.call-done = f32[512,1024]{0,1:T(8,128)} async-done(((f32[2048,1024]{0,1:T(8,128)}), f32[512,1024]{0,1:T(8,128)}) %reduce-scatter.2.cloned.1.call-update) | async-done | bytes 2097168 | tf_op jit(solution)/shard_map/reduce_scatter | solution.py:190
  625.6 2.7 convert_bitcast_fusion
  (243 shorter events, 78.5 us)
Async XLA Ops:
  7.2 95.5 %copy-start = (bf16[2048,16]{0,1:T(8,128)(2,1)S(1)}, bf16[2048,16]{0,1:T(8,128)(2,1)}, u32[]{:S(2)}) copy-start(bf16[2048,16]{0,1:T(8,128)(2,1)} %param.22) | copy-start | bytes 196612
  7.2 27.7 %all-gather.8.cloned.1.call-start = ((), (), s32[]{:S(2)}) async-start(), calls=%async_computation.2 | async-start | bytes 1310720 | tf_op jit(solution)/shard_map/all_gather | solution.py:123
  7.9 79.1 %all-gather.6.cloned.1.call-start = ((), (), s32[]{:S(2)}) async-start(), calls=%async_computation.1 | async-start | bytes 5242880 | tf_op jit(solution)/shard_map/all_gather | solution.py:124
  8.7 356.4 %all-gather.10.cloned.1.call-start = ((), (), s32[]{:S(2)}) async-start(), calls=%async_computation.5 | async-start | bytes 17301504 | tf_op jit(solution)/shard_map/all_gather | solution.py:23
  87.0 3.9 copy-start.6
  90.9 11.7 %copy-start.9 = (f32[16]{0:T(128)S(1)}, f32[16]{0:T(128)}, u32[]{:S(2)}) copy-start(f32[16]{0:T(128)} %param.25) | copy-start | bytes 196
  98.8 8.2 %collective-permute-start = (bf16[3,1280]{0,1:T(8,128)(2,1)}, bf16[3,1280]{0,1:T(8,128)(2,1)}, u32[]{:S(2)}, u32[]{:S(2)}) collective-permute-start(bf16[3,1280]{0,1:T(8,128)(2,1)} %fusion.52), channel_id=1, source_target_pairs={{0,4},{4,8},{8,12},{12,16},{16,20},{20,24},{24,28},{28,32},{32,36}... | collective-permute-start | bytes 23048 | tf_op jit(solution)/shard_map/ppermute | solution.py:18
  109.8 7.4 %copy-start.2 = (bf16[1027,1280]{0,1:T(8,128)(2,1)}, bf16[1027,1280]{0,1:T(8,128)(2,1)S(1)}, u32[]{:S(2)}) copy-start(bf16[1027,1280]{0,1:T(8,128)(2,1)S(1)} %maximum_maximum_fusion) | copy-start | bytes 7887364
  117.2 1.5 copy-start.5
  127.2 165.7 %copy-start.10 = (s32[4]{0:T(128)S(1)}, s32[4]{0:T(128)}, u32[]{:S(2)}) copy-start(s32[4]{0:T(128)} %param.30) | copy-start | bytes 52
  289.9 0.8 copy-start.4
  290.7 293.6 %all-reduce.4.cloned.1.call-start = ((), (), s32[]{:S(2)}) async-start(), calls=%async_computation.4 | async-start | bytes 4194304 | tf_op jit(solution)/shard_map/psum | solution.py:227
  330.4 72.4 %copy-start.11 = (f32[16]{0:T(128)S(1)}, f32[16]{0:T(128)}, u32[]{:S(2)}) copy-start(f32[16]{0:T(128)} %param.27) | copy-start | bytes 196
  402.8 5.9 copy-start.7
  402.8 6.0 copy-start.12
  424.6 12.0 %copy-start.8 = (f32[1024]{0:T(1024)S(1)}, f32[1024]{0:T(1024)}, u32[]{:S(2)}) copy-start(f32[1024]{0:T(1024)} %param.28) | copy-start | bytes 12292
  436.4 189.2 %reduce-scatter.2.cloned.1.call-start = ((), (), s32[]{:S(2)}) async-start(), calls=%async_computation.3 | async-start | bytes 10485760 | tf_op jit(solution)/shard_map/reduce_scatter | solution.py:190
  448.0 1.9 copy-start.3
  448.9 179.4 %copy-start.1 = (bf16[2048,16]{0,1:T(8,128)(2,1)S(1)}, bf16[2048,16]{0,1:T(8,128)(2,1)}, u32[]{:S(2)}) copy-start(bf16[2048,16]{0,1:T(8,128)(2,1)} %param.22) | copy-start | bytes 196612
Sparse Core Ops, SparseCore 0:
  9.7 25.1 all-gather.7
  36.5 50.4 all-gather.5
  290.9 74.1 all-gather.9
  436.5 106.7 all-reduce.3
  545.6 79.9 reduce-scatter.1
where the time goes:
time: 647 us; the launch traced here: 635 us
  blocking collectives  155 us (24%)
  waiting for transfers between devices  153 us (24%)
  local copies, waits for them, and re-layouts  152 us (23%)
  matrix products  78.5 us (12%)
  other arithmetic  69.2 us (11%)
  between operations  15.9 us (2%)
  loops' own time  7.02 us (1%)
    psum x1, blocking collectives, per_device(): finals_all, edges_all = lax.psum((finals, edges), 'seq')  122 us
    dynamic_update_slice x8, local copies, waits for them, and re-layouts, per_device(): local_end, (outputs, priors) = lax.scan(advance_block, init_state, packed)  98.1 us
    all_gather x1, waiting for transfers between devices, per_device(): piece = lax.all_gather(hidden, 'tp', axis=1, tiled=True)  52.1 us
    reduce_scatter x1, waiting for transfers between devices, per_device(): lax.psum_scatter(lax.dot_general(out_weight, normed, (((0,), (1,)), ((),...  39.4 us
    select_n x31, other arithmetic, lap(): jnp.where(position < mine, new, old)  36.4 us
    all_gather x1, waiting for transfers between devices, prefix(): pieces = jax.tree.map(lambda part: lax.all_gather(part, axis), value)  34.7 us
    all_gather x1, blocking collectives, prefix(): pieces = jax.tree.map(lambda part: lax.all_gather(part, axis), value)  24.6 us
    all_gather x1, waiting for transfers between devices, per_device(): bc_full = lax.all_gather(bc_weight, 'tp', axis=1, tiled=True)  22.5 us
  transfers between devices with their start and end apart: 6, of which 5 were waited for; matrix products, arithmetic and copies ran while one was open for 7% of the time, Pallas kernels for 0%

commit v1 on v0

--- a/solution.py
+++ b/solution.py
@@ -120,7 +120,9 @@
     prompt_start = prompt_end - lengths
     positions = first_row + jnp.arange(rows_here, dtype=jnp.int32)
     segment = segment_of(positions, prompt_end)
-    bc_full = lax.all_gather(bc_weight, "tp", axis=1, tiled=True)
+    bc_full = jnp.concatenate(
+        lax.all_to_all(jnp.stack([bc_weight] * lax.axis_size("tp")), "tp", 0, 0), axis=1
+    )
     piece = lax.all_gather(hidden, "tp", axis=1, tiled=True)
 
     def take(matrix):

time: 647 us -> 624 us (0.964)
  waiting for transfers between devices: 153 us -> 125 us
    all_gather x1 -> x0, waiting for transfers between devices: 22.5 us -> none  [per_device(): bc_full = lax.all_gather(bc_weight, 'tp', axis=1, tiled=True)]
    all_gather x1, waiting for transfers between devices: 52.1 us -> 34 us  [per_device(): piece = lax.all_gather(hidden, 'tp', axis=1, tiled=True)]
    all_to_all x0 -> x1, waiting for transfers between devices: none -> 14.7 us  [per_device(): lax.all_to_all(jnp.stack([bc_weight] * lax.axis_size('tp')), 'tp', 0, 0)]
where the time goes in v1:
time: 624 us; the launch traced here: 612 us
  blocking collectives  156 us (25%)
  local copies, waits for them, and re-layouts  153 us (25%)
  waiting for transfers between devices  125 us (20%)
  matrix products  78.3 us (13%)
  other arithmetic  67.8 us (11%)
  between operations  16 us (3%)
  starting transfers between devices  8.74 us (1%)
  loops' own time  6.92 us (1%)
    psum x1, blocking collectives, per_device(): finals_all, edges_all = lax.psum((finals, edges), 'seq')  122 us
    dynamic_update_slice x8, local copies, waits for them, and re-layouts, per_device(): local_end, (outputs, priors) = lax.scan(advance_block, init_state, packed)  98.1 us
    reduce_scatter x1, waiting for transfers between devices, per_device(): lax.psum_scatter(lax.dot_general(out_weight, normed, (((0,), (1,)), ((),...  39.4 us
    select_n x31, other arithmetic, lap(): jnp.where(position < mine, new, old)  36.4 us
    all_gather x1, waiting for transfers between devices, per_device(): piece = lax.all_gather(hidden, 'tp', axis=1, tiled=True)  34 us
    all_gather x1, waiting for transfers between devices, prefix(): pieces = jax.tree.map(lambda part: lax.all_gather(part, axis), value)  33.6 us
    all_gather x1, blocking collectives, prefix(): pieces = jax.tree.map(lambda part: lax.all_gather(part, axis), value)  25.6 us
    dot_general x4, matrix products, advance_block(): output = jnp.einsum('ijh,jhp->ihp', mixing, x_blk, precision=highest)  19.7 us
  transfers between devices with their start and end apart: 6, of which 5 were waited for; matrix products, arithmetic and copies ran while one was open for 7% of the time, Pallas kernels for 0%

profile of v1, /device:TPU:1, one launch (start us, length us, event | category | flops | bytes accessed | tf_op | source)
XLA Modules:
  0.0 611.7 jit_solution(8621752966474387888)
XLA Ops:
  8.0 2.0 stack.2
  10.0 4.8 all-to-all-start
  15.8 14.7 %all-to-all-done = bf16[4,2048,64]{1,2,0:T(8,128)(2,1)S(1)} async-done(((bf16[4,2048,64]{1,2,0:T(8,128)(2,1)}), bf16[4,2048,64]{1,2,0:T(8,128)(2,1)S(1)}, u32[]{:S(2)}, u32[]{:S(2)}) %all-to-all-start) | async-done | bytes 1048608 | tf_op jit(solution)/shard_map/all_to_all | solution.py:124
  30.5 34.0 %all-gather.5.cloned.1.call-done = bf16[1024,2048]{1,0:T(8,128)(2,1)} async-done(((bf16[1024,512]{1,0:T(8,128)(2,1)}), bf16[1024,2048]{1,0:T(8,128)(2,1)}) %all-gather.5.cloned.1.call-update) | async-done | bytes 4194320 | tf_op jit(solution)/shard_map/all_gather | solution.py:126
  64.4 3.7 convolution_convert_fusion.1
  68.2 7.0 %convolution_convert_fusion = bf16[1024,1024]{0,1:T(8,128)(2,1)S(1)} fusion(bf16[1024,2048]{1,0:T(8,128)(2,1)S(1)} %copy-done.6, bf16[2048,1024]{1,0:T(8,128)(2,1)} %param.19), kind=kOutput, calls=%fused_computation.87 | convolution fusion | flops 4296015872 | bytes 10485760 | tf_op jit(solution)/shard_map/dot_general | solution.py:129
  76.1 3.6 collective-permute-start
  81.0 3.0 collective-permute-done
  84.0 2.8 maximum_maximum_fusion
  86.8 7.4 %multiply_convert_fusion = bf16[1024,1280]{0,1:T(8,128)(2,1)S(1)} fusion(bf16[1024,256]{0,1:T(8,128)(2,1)S(1)} %convolution_convert_fusion.1, bf16[1027,1280]{0,1:T(8,128)(2,1)S(1)} %maximum_maximum_fusion, f32[1280]{0:T(1024)S(1)} %get-tuple-element.304, f32[1024]{0:T(1024)S(1)} %get-tuple-element.360, f32[1280]{0:T(1024)S(1)} %get-tuple-element.305, ...), kind=kLoop, calls=%fused_computation.69 | loop fusion | flops 28835840 | bytes 13139968 | tf_op jit(solution)/shard_map/convert_element_type | solution.py:52
  94.3 1.4 copy-done.5
  95.7 2.4 slice_convert_fusion
  98.6 5.6 reshape_reshape.3
  104.2 162.3 %while.32 = (s32[]{:T(128)}, f32[16,64,128]{2,1,0:T(8,128)S(1)}, f32[4,256,16,64]{1,0,3,2:T(4,128)}, s32[4,256]{1,0:T(4,128)S(1)}, s32[4]{0:T(128)S(1)}, /*index...) while((s32[]{:T(128)}, f32[16,64,128]{2,1,0:T(8,128)S(1)}, ...), condition=%wide.region_7.8_spmd.clone.clone, body=%wide.region_4.7_spmd.clone.sunk.clone | while | flops 1718571520 | bytes 14622798 | solution.py:169
  107.0 1.3 broadcast_compare_fusion.6
  110.0 3.3 constant_dynamic-slice_fusion.14
  113.3 4.9 fusion.121
  121.5 23.4 %dynamic_update_slice.7 = f32[4,256,16,64]{1,0,3,2:T(4,128)} dynamic-update-slice(f32[4,256,16,64]{1,0,3,2:T(4,128)} %get-tuple-element.565, f32[1,256,16,64]{1,0,3,2:T(1,128)S(1)} %copy.169, s32[]{:T(128)S(6)} %copy.176, s32[]{:T(128)} %constant.101.clone.1..sunk.2, s32[]{:T(128)} %constant.101.clone.1..sunk.2, s32[]{:T(128)} %constant.101.clone.1..sunk.2) | dynamic-update-slice | bytes 2097156 | tf_op jit(solution)/shard_map/while/body/jit(dynamic_update_index_in_dim)/dynamic_update_slice | solution.py:169
  147.5 1.3 broadcast_compare_fusion.6
  150.5 3.3 constant_dynamic-slice_fusion.14
  153.8 4.9 fusion.121
  162.0 23.4 %dynamic_update_slice.7 = f32[4,256,16,64]{1,0,3,2:T(4,128)} dynamic-update-slice(f32[4,256,16,64]{1,0,3,2:T(4,128)} %get-tuple-element.565, f32[1,256,16,64]{1,0,3,2:T(1,128)S(1)} %copy.169, s32[]{:T(128)S(6)} %copy.176, s32[]{:T(128)} %constant.101.clone.1..sunk.2, s32[]{:T(128)} %constant.101.clone.1..sunk.2, s32[]{:T(128)} %constant.101.clone.1..sunk.2) | dynamic-update-slice | bytes 2097156 | tf_op jit(solution)/shard_map/while/body/jit(dynamic_update_index_in_dim)/dynamic_update_slice | solution.py:169
  191.0 3.3 constant_dynamic-slice_fusion.14
  194.3 4.9 fusion.121
  202.5 23.4 %dynamic_update_slice.7 = f32[4,256,16,64]{1,0,3,2:T(4,128)} dynamic-update-slice(f32[4,256,16,64]{1,0,3,2:T(4,128)} %get-tuple-element.565, f32[1,256,16,64]{1,0,3,2:T(1,128)S(1)} %copy.169, s32[]{:T(128)S(6)} %copy.176, s32[]{:T(128)} %constant.101.clone.1..sunk.2, s32[]{:T(128)} %constant.101.clone.1..sunk.2, s32[]{:T(128)} %constant.101.clone.1..sunk.2) | dynamic-update-slice | bytes 2097156 | tf_op jit(solution)/shard_map/while/body/jit(dynamic_update_index_in_dim)/dynamic_update_slice | solution.py:169
  231.5 3.3 constant_dynamic-slice_fusion.14
  234.8 4.9 fusion.121
  243.0 23.4 %dynamic_update_slice.7 = f32[4,256,16,64]{1,0,3,2:T(4,128)} dynamic-update-slice(f32[4,256,16,64]{1,0,3,2:T(4,128)} %get-tuple-element.565, f32[1,256,16,64]{1,0,3,2:T(1,128)S(1)} %copy.169, s32[]{:T(128)S(6)} %copy.176, s32[]{:T(128)} %constant.101.clone.1..sunk.2, s32[]{:T(128)} %constant.101.clone.1..sunk.2, s32[]{:T(128)} %constant.101.clone.1..sunk.2) | dynamic-update-slice | bytes 2097156 | tf_op jit(solution)/shard_map/while/body/jit(dynamic_update_index_in_dim)/dynamic_update_slice | solution.py:169
  269.6 4.5 reduce-window.21
  275.8 25.6 %all-gather.1 = f32[32,1,16]{2,1,0:T(1,128)S(1)} all-gather(f32[1,1,16]{2,1,0:T(1,128)S(1)} %bitcast.256), channel_id=1, replica_groups=mesh['seq'=32,'tp'=4] {'seq'}, dimensions={0}, use_global_device_ids=true | all-gather | bytes 2112 | tf_op jit(solution)/shard_map/all_gather | solution.py:23
  301.5 6.5 %reshape.372 = f32[1024,16,64]{0,2,1:T(8,128)} reshape(f32[4,256,16,64]{1,0,3,2:T(4,128)} %get-tuple-element.151) | data formatting | bytes 8388608 | tf_op jit(solution)/shard_map/reshape | solution.py:184
  308.1 33.6 %all-gather.7.cloned.1.call-done = f32[512,64,128]{2,1,0:T(8,128)} async-done(((f32[16,64,128]{2,1,0:T(8,128)}), f32[512,64,128]{2,1,0:T(8,128)}) %all-gather.7.cloned.1.call-update) | async-done | bytes 16777232 | tf_op jit(solution)/shard_map/all_gather | solution.py:23
  341.7 37.7 %while.33 = (s32[]{:T(128)}, f32[16,64,128]{2,1,0:T(8,128)S(1)}, s32[]{:T(128)}, f32[32,16]{1,0:T(8,128)S(1)}, f32[32,16,64,128]{3,2,1,0:T(8,128)}) while((s32[]{:T(128)}, f32[16,64,128]{2,1,0:T(8,128)S(1)}, s32[]{:T(128)}, f32[32,16]{1,0:T(8,128)S(1)}, f32[32,16,64,128]{3,2,1,0:T(8,128)}) %tuple.134), condition=%wide.region_11.12_spmd.clone.clone, body=%wide.region_10.11_spmd.clone.sunk.clone | while | flops 524292 | bytes 1573153 | solution.py:32
  379.5 5.9 multiply_add_fusion
  385.4 7.3 %multiply_reduce_fusion = (f32[1024]{0:T(1024)S(1)}, f32[1024,1024]{0,1:T(8,128)}) fusion(bf16[1024,2048]{1,0:T(8,128)(2,1)S(1)} %copy-done.7, bf16[2048,1024]{1,0:T(8,128)(2,1)S(1)} %copy-done.14, f32[1024,16,64]{0,2,1:T(8,128)S(1)} %multiply_add_fusion), kind=kOutput, calls=%fused_computation.76 | convolution fusion | flops 4304403456 | bytes 16781312 | tf_op jit(solution)/shard_map/dot_general | solution.py:129
  392.7 8.5 %psum.21 = f32[1024]{0:T(1024)S(1)} all-reduce(f32[1024]{0:T(1024)S(1)} %get-tuple-element.368), channel_id=1, replica_groups=mesh['seq'=32,'tp'=4] {'tp'}, use_global_device_ids=true, to_apply=%region_13.14 | all-reduce | flops 1024 | bytes 8192 | tf_op jit(solution)/shard_map/psum | solution.py:188
  401.3 11.7 %fusion.47 = f32[4,16,64,128]{3,2,0,1:T(8,128)} fusion(f32[1024,16,64]{0,2,1:T(8,128)} %bitcast.237, f32[1024,16,4]{0,2,1:T(4,128)S(1)} %multiply_bitcast_fusion, f32[16,64,128]{2,1,0:T(8,128)S(1)} %get-tuple-element.153, f32[4,16]{0,1:T(8,128)S(1)} %copy.102, pred[4]{0:T(512)(128)(4,1)S(1)} %fusion.76, bf16[1024,1280]{0,1:T(8,128)(2,1)} %copy-done.5), kind=kOutput, calls=%fused_computation.84 | convolution fusion | flops 6448218112 | bytes 7340292 | tf_op jit(solution)/shard_map/vmap(jh,jhp,jn->hpn)/dot_general | solution.py:92
  413.3 11.4 %convolution_bitcast_fusion = f32[2048,1024]{0,1:T(8,128)} fusion(bf16[1024,2048]{1,0:T(8,128)(2,1)} %param.29, f32[1024,1024]{0,1:T(8,128)} %get-tuple-element.369, f32[1024]{0:T(1024)S(1)} %copy-done.8, f32[1024]{0:T(1024)S(1)} %add_rsqrt_fusion), kind=kOutput, calls=%fused_computation.70 | convolution fusion | flops 4298113024 | bytes 16785408 | tf_op jit(solution)/shard_map/dot_general | solution.py:193
  426.5 3.4 copy.105
  429.9 8.0 %while.31 = (s32[]{:T(128)}, bf16[1027,1280]{1,0:T(8,128)(2,1)}, s32[4,2]{0,1:T(2,128)S(1)}, bf16[4,3,1280]{2,1,0:T(4,128)(2,1)S(1)}) while((s32[]{:T(128)}, bf16[1027,1280]{1,0:T(8,128)(2,1)}, s32[4,2]{0,1:T(2,128)S(1)}, bf16[4,3,1280]{2,1,0:T(4,128)(2,1)S(1)}) %tuple.120), condition=%wide.while_cond.clone, body=%wide.while_body.sunk.clone | while | flops 2 | bytes 18017 | solution.py:223
  430.5 1.4 bitcast_dynamic-update-slice_fusion.3
  432.5 1.4 bitcast_dynamic-update-slice_fusion.3
  434.5 1.4 bitcast_dynamic-update-slice_fusion.3
  436.5 1.4 bitcast_dynamic-update-slice_fusion.3
  438.0 121.7 %psum.23 = bf16[4,3,1280]{2,1,0:T(4,128)(2,1)S(1)} all-reduce(f32[4,3,1280]{2,1,0:T(4,128)S(1)} %convert_select_fusion), channel_id=1, replica_groups=mesh['seq'=32,'tp'=4] {'seq'}, use_global_device_ids=true, to_apply=%region_16.17 | all-reduce | flops 15360 | bytes 92160 | tf_op jit(solution)/shard_map/psum | solution.py:229
  560.9 1.9 dynamic-slice_bitcast_fusion.1
  562.8 39.4 %reduce-scatter.2.cloned.1.call-done = f32[512,1024]{0,1:T(8,128)} async-done(((f32[2048,1024]{0,1:T(8,128)}), f32[512,1024]{0,1:T(8,128)}) %reduce-scatter.2.cloned.1.call-update) | async-done | bytes 2097168 | tf_op jit(solution)/shard_map/reduce_scatter | solution.py:192
  602.2 2.7 convert_bitcast_fusion
  (249 shorter events, 77.4 us)
Async XLA Ops:
  7.2 72.5 %copy-start = (bf16[2048,16]{0,1:T(8,128)(2,1)S(1)}, bf16[2048,16]{0,1:T(8,128)(2,1)}, u32[]{:S(2)}) copy-start(bf16[2048,16]{0,1:T(8,128)(2,1)} %param.22) | copy-start | bytes 196612
  7.2 7.7 %copy-start.12 = (s32[4]{0:T(128)S(1)}, s32[4]{0:T(128)}, u32[]{:S(2)}) copy-start(s32[4]{0:T(128)} %param.30) | copy-start | bytes 52
  7.2 7.8 %copy-start.15 = (f32[16]{0:T(128)S(1)}, f32[16]{0:T(128)}, u32[]{:S(2)}) copy-start(f32[16]{0:T(128)} %param.26) | copy-start | bytes 196
  7.2 8.0 %copy-start.9 = (f32[4,1024]{1,0:T(4,128)S(1)}, f32[4,1024]{1,0:T(4,128)}, u32[]{:S(2)}) copy-start(f32[4,1024]{1,0:T(4,128)} %param.23) | copy-start | bytes 49156
  7.2 8.0 %copy-start.10 = (f32[4,256]{1,0:T(4,128)S(1)}, f32[4,256]{1,0:T(4,128)}, u32[]{:S(2)}) copy-start(f32[4,256]{1,0:T(4,128)} %param.24) | copy-start | bytes 12292
  7.2 57.2 %all-gather.5.cloned.1.call-start = ((), (), s32[]{:S(2)}) async-start(), calls=%async_computation.2 | async-start | bytes 5242880 | tf_op jit(solution)/shard_map/all_gather | solution.py:126
  10.0 20.5 %all-to-all-start = ((bf16[4,2048,64]{1,2,0:T(8,128)(2,1)}), bf16[4,2048,64]{1,2,0:T(8,128)(2,1)S(1)}, u32[]{:S(2)}, u32[]{:S(2)}) async-start(bf16[4,2048,64]{1,2,0:T(8,128)(2,1)} %stack.2), calls=%async_computation | async-start | bytes 2097152 | tf_op jit(solution)/shard_map/all_to_all | solution.py:124
  14.8 326.9 %all-gather.7.cloned.1.call-start = ((), (), s32[]{:S(2)}) async-start(), calls=%async_computation.5 | async-start | bytes 17301504 | tf_op jit(solution)/shard_map/all_gather | solution.py:23
  64.4 3.8 copy-start.6
  68.2 11.5 %copy-start.11 = (f32[16]{0:T(128)S(1)}, f32[16]{0:T(128)}, u32[]{:S(2)}) copy-start(f32[16]{0:T(128)} %param.25) | copy-start | bytes 196
  76.1 7.9 %collective-permute-start = (bf16[3,1280]{0,1:T(8,128)(2,1)}, bf16[3,1280]{0,1:T(8,128)(2,1)}, u32[]{:S(2)}, u32[]{:S(2)}) collective-permute-start(bf16[3,1280]{0,1:T(8,128)(2,1)} %fusion.52), channel_id=1, source_target_pairs={{0,4},{4,8},{8,12},{12,16},{16,20},{20,24},{24,28},{28,32},{32,36}... | collective-permute-start | bytes 23048 | tf_op jit(solution)/shard_map/ppermute | solution.py:18
  86.8 7.4 %copy-start.2 = (bf16[1027,1280]{0,1:T(8,128)(2,1)}, bf16[1027,1280]{0,1:T(8,128)(2,1)S(1)}, u32[]{:S(2)}) copy-start(bf16[1027,1280]{0,1:T(8,128)(2,1)S(1)} %maximum_maximum_fusion) | copy-start | bytes 7887364
  94.2 1.5 copy-start.5
  266.5 0.8 copy-start.4
  267.3 293.6 %all-reduce.4.cloned.1.call-start = ((), (), s32[]{:S(2)}) async-start(), calls=%async_computation.4 | async-start | bytes 4194304 | tf_op jit(solution)/shard_map/psum | solution.py:229
  308.1 71.4 %copy-start.13 = (f32[16]{0:T(128)S(1)}, f32[16]{0:T(128)}, u32[]{:S(2)}) copy-start(f32[16]{0:T(128)} %param.27) | copy-start | bytes 196
  379.4 5.9 copy-start.7
  379.4 6.0 copy-start.14
  401.2 12.0 %copy-start.8 = (f32[1024]{0:T(1024)S(1)}, f32[1024]{0:T(1024)}, u32[]{:S(2)}) copy-start(f32[1024]{0:T(1024)} %param.28) | copy-start | bytes 12292
  413.0 189.2 %reduce-scatter.2.cloned.1.call-start = ((), (), s32[]{:S(2)}) async-start(), calls=%async_computation.3 | async-start | bytes 10485760 | tf_op jit(solution)/shard_map/reduce_scatter | solution.py:192
  424.7 1.9 copy-start.3
  425.5 179.4 %copy-start.1 = (bf16[2048,16]{0,1:T(8,128)(2,1)S(1)}, bf16[2048,16]{0,1:T(8,128)(2,1)}, u32[]{:S(2)}) copy-start(bf16[2048,16]{0,1:T(8,128)(2,1)} %param.22) | copy-start | bytes 196612
Sparse Core Ops, SparseCore 0:
  9.7 54.6 all-gather.4
  267.4 74.2 all-gather.6
  413.1 106.6 all-reduce.3
  522.2 80.0 reduce-scatter.1
